TPU v7x, 512 devices: a whole 4x4x16 slice. The times are simulated.
512 devices in a mesh: pool: 128 (over x, z, core), tp: 4 (over y).
Axes of the slice: x: 4, y: 4, z: 16, core: 2. Of those that a mesh axis runs over, the one named last changes fastest.
Arguments:
- hidden_rows: bfloat16 [16384, 8192], P('pool', 'tp'), may hold values from -6 to 6
- kv_weight: bfloat16 [8192, 1024], P('tp', 'pool'), may hold values from -0.0625 to 0.0625
- queries: bfloat16 [16384, 4096], P('pool', 'tp'), may hold values from -5 to 5
- cache_table: bfloat16 [1024, 128, 1024], P('pool', None, 'tp'), may hold values from -5 to 5
- retrieval: int32 [128, 64], P('pool'), may hold values from 0 to 1023, as said below
- pattern: int32 [128, 2, 64], P('pool'), may hold values 0 or 1
Outputs:
- attended: bfloat16 [16384, 4096], P('pool', 'tp')
- fresh_kv: bfloat16 [16384, 1024], P('pool', 'tp')
Inputs may be any that keep to these rules, and one draw needn't show every extreme that they name: `retrieval`: each request names 64 blocks held by 64 different devices (block b is held by device b // 8); one device, drawn from the seed, holds a block named by every request.
All inputs are finite; a program needn't handle non-finite values. No bound on the sum of `pattern` on one device may be relied on, other than what follows from the above.
Results may differ from a plain program's by a relative error of at most 0.025.
Values may be sent and summed in bfloat16 or wider, within the bound.
No kernel may reach another device: no remote copies, remote signals or barrier semaphores. Data moves between devices by JAX's collectives and lax.ppermute only.
A program may use at most 192 MiB of HBM per device.

v0:
```python
import math
import jax
import jax.numpy as jnp
from jax import lax
from jax.sharding import PartitionSpec as P

HD = 128
QH = 32
KVH = 4
BLK = 128
RBLK = 64


def rows_by_keys(left, right):
    return lax.dot_general(
        left, right, (((1,), (1,)), ((), ())), preferred_element_type=jnp.float32
    )


def body(hidden_rows, kv_weight, queries, cache_table, retrieval, pattern):
    partial_kv = jnp.dot(
        hidden_rows,
        lax.all_gather(kv_weight, "pool", axis=1, tiled=True),
        preferred_element_type=jnp.float32,
    )
    fresh = lax.psum_scatter(partial_kv.astype(jnp.bfloat16), "tp", scatter_dimension=1, tiled=True)
    wanted = retrieval[0]
    npool = lax.axis_size("pool")
    by_token = lax.all_to_all(cache_table, "pool", split_axis=1, concat_axis=0, tiled=True)
    by_token = by_token.reshape(by_token.shape[0], by_token.shape[2])
    wanted_all = lax.all_gather(retrieval, "pool", axis=0, tiled=True)
    reply = jnp.take(by_token, wanted_all, axis=0)
    fetched = lax.all_to_all(reply[:, :, None, :], "pool", split_axis=0, concat_axis=2, tiled=True)[
        0
    ]
    count = hidden_rows.shape[0]
    fetch_count = wanted.shape[0]
    group = QH // KVH
    scale = float(HD) ** (-0.5)
    local_heads = fresh.shape[1] // (2 * HD)
    width = fetched.shape[2]
    per_step = math.gcd(fetch_count, 8)
    steps_count = fetch_count // per_step
    grouped = fetched.reshape(steps_count, per_step * BLK, width)
    pat_steps = jnp.transpose(
        pattern[0].reshape(pattern.shape[1], steps_count, per_step), (1, 0, 2)
    )
    token_of_row = jnp.arange(count * group) // group
    block_of_row = token_of_row // RBLK
    row_blocks = block_of_row[:, None, None] == jnp.arange(pattern.shape[1])[None, :, None]
    near_mask = token_of_row[:, None] >= jnp.arange(count)[None, :]
    q_heads = queries.reshape(count, local_heads, group * HD)
    q_rows = q_heads[:, 0].reshape(count * group, HD)
    near_keys = fresh[:, 0:HD]
    near_vals = fresh[:, HD : 2 * HD]
    near_scores = rows_by_keys(q_rows, near_keys) * scale
    top = jnp.max(jnp.where(near_mask, near_scores, -1e30), axis=1)
    weights = jnp.where(near_mask, jnp.exp(near_scores - top[:, None]), 0.0)
    total = jnp.sum(weights, axis=1)
    numer = jnp.dot(weights.astype(jnp.bfloat16), near_vals, preferred_element_type=jnp.float32)

    def visit(carry, items):
        top_now, total_now, numer_now = carry
        block_rows, pat_now = items
        keys = block_rows[:, 0:HD]
        vals = block_rows[:, HD : 2 * HD]
        scores = rows_by_keys(q_rows, keys) * scale
        row_pat = jnp.any(row_blocks & (pat_now[None] != 0), axis=1)
        mask = jnp.repeat(row_pat, BLK, axis=1)
        top_new = jnp.maximum(top_now, jnp.max(jnp.where(mask, scores, -1e30), axis=1))
        weights_now = jnp.where(mask, jnp.exp(scores - top_new[:, None]), 0.0)
        factor = jnp.exp(top_now - top_new)
        total_new = total_now * factor + jnp.sum(weights_now, axis=1)
        numer_new = numer_now * factor[:, None] + jnp.dot(
            weights_now.astype(jnp.bfloat16), vals, preferred_element_type=jnp.float32
        )
        return ((top_new, total_new, numer_new), None)

    (top, total, numer), unused = lax.scan(visit, (top, total, numer), (grouped, pat_steps))
    results = (numer / total[:, None]).reshape(count, group * HD)
    attended = results.astype(jnp.bfloat16)
    return (attended, fresh)


def solution(mesh):
    placed = (
        P("pool", "tp"),
        P("tp", "pool"),
        P("pool", "tp"),
        P("pool", None, "tp"),
        P("pool", None),
        P("pool", None, None),
    )
    return jax.shard_map(
        body,
        mesh=mesh,
        in_specs=placed,
        out_specs=(P("pool", "tp"), P("pool", "tp")),
        check_vma=False,
    )
```

profile of v0, /device:TPU:4, one launch (start us, length us, event | category | flops | bytes accessed | tf_op | source)
XLA Modules:
  0.0 440.1 jit_solution(318980175920545042)
XLA Ops:
  7.2 2.2 copy.24
  9.4 19.7 %all-to-all-start = ((bf16[8,128,256]{2,0,1:T(8,128)(2,1)}), bf16[8,128,256]{2,0,1:T(8,128)(2,1)S(1)}, u32[]{:S(2)}, u32[]{:S(2)}) async-start(bf16[8,128,256]{2,0,1:T(8,128)(2,1)} %copy.24), calls=%async_computation.1 | async-start | bytes 1048576 | tf_op jit(solution)/shard_map/all_to_all | solution.py:29
  29.1 92.0 %all-gather = s32[128,1,64]{2,1,0:T(1,128)S(1)} all-gather(s32[1,1,64]{2,1,0:T(1,128)} %bitcast.77), channel_id=1, replica_groups=mesh['pool'=128,'tp'=4] {'pool'}, dimensions={0}, use_global_device_ids=true | all-gather | bytes 33024 | tf_op jit(solution)/shard_map/all_gather | solution.py:31
  121.2 33.1 %gather_fusion = bf16[8192,256]{1,0:T(8,128)(2,1)} fusion(bf16[1024,256]{1,0:T(8,128)(2,1)S(1)} %bitcast.70, s32[8192]{0:T(1024)S(1)} %broadcast_clamp_fusion), kind=kCustom, calls=%fused_computation | custom fusion | bytes 8421376 | tf_op jit(solution)/shard_map/jit(_take)/gather | solution.py:32
  154.4 5.2 %broadcast_select_fusion = bf16[128,64,1,256]{3,1,2,0:T(8,128)(2,1)} fusion(bf16[128,64,1,256]{3,1,2,0:T(8,128)(2,1)} %bitcast.71, pred[128,64]{1,0:T(8,128)(4,1)S(1)} %compare_and_fusion), kind=kLoop, calls=%fused_computation.20 | loop fusion | flops 2097152 | bytes 8396800 | tf_op jit(solution)/shard_map/jit(_take)/select_n | solution.py:32
  159.6 14.0 %all-to-all-start.1 = ((bf16[128,64,1,256]{3,1,2,0:T(8,128)(2,1)}), bf16[128,64,1,256]{3,1,2,0:T(8,128)(2,1)}, u32[]{:S(2)}, u32[]{:S(2)}) async-start(bf16[128,64,1,256]{3,1,2,0:T(8,128)(2,1)} %broadcast_select_fusion), calls=%async_computation.2 | async-start | bytes 8388608 | tf_op jit(solution)/shard_map/all_to_all | solution.py:33
  173.7 0.7 all-gather.3.cloned.1.call-update
  174.4 0.2 reduce-scatter.2.cloned.1.call-start
  174.6 183.9 %all-gather.3.cloned.1.call-done = bf16[2048,1024]{0,1:T(8,128)(2,1)} async-done(((bf16[2048,8]{0,1:T(8,128)(2,1)}), bf16[2048,1024]{0,1:T(8,128)(2,1)}) %all-gather.3.cloned.1.call-update) | async-done | bytes 4194320 | tf_op jit(solution)/shard_map/all_gather | solution.py:23
  358.5 4.4 %convolution_convert_fusion = bf16[128,1024]{1,0:T(8,128)(2,1)} fusion(bf16[128,2048]{1,0:T(8,128)(2,1)S(1)} %copy-done, bf16[2048,1024]{0,1:T(8,128)(2,1)} %all-gather.3.cloned.1.call-done), kind=kOutput, calls=%fused_computation.23 | convolution fusion | flops 537001984 | bytes 4980736 | tf_op jit(solution)/shard_map/dot_general | solution.py:21
  363.1 29.0 %reduce-scatter.2.cloned.1.call-done = bf16[128,256]{1,0:T(8,128)(2,1)} async-done(((bf16[128,1024]{1,0:T(8,128)(2,1)}), bf16[128,256]{1,0:T(8,128)(2,1)}) %reduce-scatter.2.cloned.1.call-update) | async-done | bytes 65552 | tf_op jit(solution)/shard_map/reduce_scatter | solution.py:26
  392.1 1.0 select_reduce_fusion
  393.3 1.0 fusion.12
  394.3 6.5 %copy.26 = bf16[128,64,1,256]{3,0,1,2:T(8,128)(2,1)} copy(bf16[128,64,1,256]{3,1,2,0:T(8,128)(2,1)} %all-to-all-done.1) | data formatting | bytes 8388608 | tf_op jit(solution)/shard_map/all_to_all | solution.py:33
  400.8 31.4 %while.15 = (s32[]{:T(128)}, f32[1024]{0:T(1024)S(1)}, f32[1024]{0:T(1024)S(1)}, f32[1024,128]{1,0:T(8,128)S(1)}, s32[8,2,8]{2,0,1:T(8,128)S(1)}, /*index=5*/bf1...) while((s32[]{:T(128)}, f32[1024]{0:T(1024)S(1)}, ...), condition=%wide.region_7.8_spmd.clone, body=%wide.region_3.7_spmd.clone.sunk | while | flops 545550336 | bytes 15561037 | solution.py:79
  400.9 1.1 dynamic-slice_bitcast_fusion.2
  402.0 0.7 fusion.38
  402.8 0.9 fusion.39
  403.7 1.0 convolution_add_fusion.2
  404.9 1.1 dynamic-slice_bitcast_fusion.2
  405.9 0.7 fusion.38
  406.7 0.9 fusion.39
  407.7 1.0 convolution_add_fusion.2
  408.8 1.1 dynamic-slice_bitcast_fusion.2
  409.9 0.7 fusion.38
  410.6 0.9 fusion.39
  411.6 1.0 convolution_add_fusion.2
  412.7 1.1 dynamic-slice_bitcast_fusion.2
  413.8 0.7 fusion.38
  414.6 0.9 fusion.39
  415.5 1.0 convolution_add_fusion.2
  416.7 1.1 dynamic-slice_bitcast_fusion.2
  417.7 0.7 fusion.38
  418.5 0.9 fusion.39
  419.5 1.0 convolution_add_fusion.2
  420.6 1.1 dynamic-slice_bitcast_fusion.2
  421.7 0.7 fusion.38
  422.4 0.9 fusion.39
  423.4 1.0 convolution_add_fusion.2
  424.5 1.1 dynamic-slice_bitcast_fusion.2
  425.6 0.7 fusion.38
  426.4 0.9 fusion.39
  427.3 1.0 convolution_add_fusion.2
  428.5 1.1 dynamic-slice_bitcast_fusion.2
  429.5 0.7 fusion.38
  430.3 0.9 fusion.39
  431.3 1.0 convolution_add_fusion.2
  432.5 0.8 convert_element_type.18
  (76 shorter events, 1.7 us)
Async XLA Ops:
  7.2 351.3 %copy-start = (bf16[128,2048]{1,0:T(8,128)(2,1)S(1)}, bf16[128,2048]{1,0:T(8,128)(2,1)}, u32[]{:S(2)}) copy-start(bf16[128,2048]{1,0:T(8,128)(2,1)} %param.8) | copy-start | bytes 1572868
  9.4 111.9 %all-to-all-start = ((bf16[8,128,256]{2,0,1:T(8,128)(2,1)}), bf16[8,128,256]{2,0,1:T(8,128)(2,1)S(1)}, u32[]{:S(2)}, u32[]{:S(2)}) async-start(bf16[8,128,256]{2,0,1:T(8,128)(2,1)} %copy.24), calls=%async_computation.1 | async-start | bytes 1048576 | tf_op jit(solution)/shard_map/all_to_all | solution.py:29
  159.6 234.7 %all-to-all-start.1 = ((bf16[128,64,1,256]{3,1,2,0:T(8,128)(2,1)}), bf16[128,64,1,256]{3,1,2,0:T(8,128)(2,1)}, u32[]{:S(2)}, u32[]{:S(2)}) async-start(bf16[128,64,1,256]{3,1,2,0:T(8,128)(2,1)} %broadcast_select_fusion), calls=%async_computation.2 | async-start | bytes 8388608 | tf_op jit(solution)/shard_map/all_to_all | solution.py:33
  173.6 189.3 %copy-start.2 = (s32[1,2,64]{2,1,0:T(2,128)S(1)}, s32[1,2,64]{2,1,0:T(2,128)}, u32[]{:S(2)}) copy-start(s32[1,2,64]{2,1,0:T(2,128)} %param.13) | copy-start | bytes 1540
  173.6 189.4 %copy-start.1 = (bf16[128,1024]{1,0:T(8,128)(2,1)S(1)}, bf16[128,1024]{1,0:T(8,128)(2,1)}, u32[]{:S(2)}) copy-start(bf16[128,1024]{1,0:T(8,128)(2,1)} %param.10) | copy-start | bytes 786436
  173.6 184.8 %all-gather.3.cloned.1.call-start = ((), (), s32[]{:S(2)}) async-start(), calls=%async_computation.3 | async-start | bytes 4227072 | tf_op jit(solution)/shard_map/all_gather | solution.py:23
  174.4 217.8 %reduce-scatter.2.cloned.1.call-start = ((), (), s32[]{:S(2)}) async-start(), calls=%async_computation.4 | async-start | bytes 327680 | tf_op jit(solution)/shard_map/reduce_scatter | solution.py:26
Sparse Core Ops, SparseCore 0:
  177.6 180.8 all-gather.2
  363.0 29.0 reduce-scatter.1
where the time goes:
time: 441 us; the launch traced here: 440 us
  waiting for transfers between devices  214 us (49%)
  blocking collectives  92 us (21%)
  local copies, waits for them, and re-layouts  51.6 us (12%)
  starting transfers between devices  34 us (8%)
  matrix products  20.2 us (5%)
  between operations  14.2 us (3%)
  other arithmetic  14 us (3%)
    all_gather x1, waiting for transfers between devices, body(): lax.all_gather(kv_weight, 'pool', axis=1, tiled=True)  184 us
    all_gather x1, blocking collectives, body(): wanted_all = lax.all_gather(retrieval, 'pool', axis=0, tiled=True)  92 us
    gather x1, local copies, waits for them, and re-layouts, body(): reply = jnp.take(by_token, wanted_all, axis=0)  33.1 us
    reduce_scatter x1, waiting for transfers between devices, body(): lax.psum_scatter(partial_kv.astype(jnp.bfloat16), 'tp', scatter_dimension...  29 us
    all_to_all x1, starting transfers between devices, body(): lax.all_to_all(cache_table, 'pool', split_axis=1, concat_axis=0, tiled=True)  19.7 us
    all_to_all x1, starting transfers between devices, body(): lax.all_to_all(reply[:, :, None, :], 'pool', split_axis=0, concat_axis=2,...  14 us
  transfers between devices with their start and end apart: 4, of which 2 were waited for; matrix products, arithmetic and copies ran while one was open for 2% of the time, Pallas kernels for 0%

commit v1 on v0

--- a/solution.py
+++ b/solution.py
@@ -30,9 +30,12 @@
     by_token = by_token.reshape(by_token.shape[0], by_token.shape[2])
     wanted_all = lax.all_gather(retrieval, "pool", axis=0, tiled=True)
     reply = jnp.take(by_token, wanted_all, axis=0)
-    fetched = lax.all_to_all(reply[:, :, None, :], "pool", split_axis=0, concat_axis=2, tiled=True)[
-        0
-    ]
+    fetched = jnp.concatenate(
+        lax.all_to_all(
+            jnp.stack(jnp.split(reply[:, :, None, :], lax.axis_size("pool"), axis=0)), "pool", 0, 0
+        ),
+        axis=2,
+    )[0]
     count = hidden_rows.shape[0]
     fetch_count = wanted.shape[0]
     group = QH // KVH

time: 441 us -> 519 us (1.18)
  the two profiles are of different devices: /device:TPU:4 before, /device:TPU:2 now
where the time goes in v1:
time: 519 us; the launch traced here: 518 us
  waiting for transfers between devices  214 us (41%)
  local copies, waits for them, and re-layouts  130 us (25%)
  blocking collectives  95.1 us (18%)
  starting transfers between devices  30.7 us (6%)
  matrix products  20.2 us (4%)
  between operations  14.2 us (3%)
  other arithmetic  13.1 us (3%)
    all_gather x1, waiting for transfers between devices, body(): lax.all_gather(kv_weight, 'pool', axis=1, tiled=True)  184 us
    all_gather x1, blocking collectives, body(): wanted_all = lax.all_gather(retrieval, 'pool', axis=0, tiled=True)  95.1 us
    unnamed x134, local copies, waits for them, and re-layouts  80 us
    gather x1, local copies, waits for them, and re-layouts, body(): reply = jnp.take(by_token, wanted_all, axis=0)  33.1 us
    reduce_scatter x1, waiting for transfers between devices, body(): lax.psum_scatter(partial_kv.astype(jnp.bfloat16), 'tp', scatter_dimension...  28.9 us
    all_to_all x1, starting transfers between devices, body(): lax.all_to_all(cache_table, 'pool', split_axis=1, concat_axis=0, tiled=True)  19.5 us
    all_to_all x1, starting transfers between devices, body(): lax.all_to_all(jnp.stack(jnp.split(reply[:, :, None, :], lax.axis_size('p...  10.9 us
  transfers between devices with their start and end apart: 4, of which 2 were waited for; matrix products, arithmetic and copies ran while one was open for 1% of the time, Pallas kernels for 0%

profile of v1, /device:TPU:2, one launch (start us, length us, event | category | flops | bytes accessed | tf_op | source)
XLA Modules:
  0.0 517.7 jit_solution(1415827210770720806)
XLA Ops:
  7.2 2.2 copy.19
  9.4 19.5 %all-to-all-start = ((bf16[8,128,256]{2,0,1:T(8,128)(2,1)}), bf16[8,128,256]{2,0,1:T(8,128)(2,1)S(1)}, u32[]{:S(2)}, u32[]{:S(2)}) async-start(bf16[8,128,256]{2,0,1:T(8,128)(2,1)} %copy.19), calls=%async_computation.1 | async-start | bytes 1048576 | tf_op jit(solution)/shard_map/all_to_all | solution.py:29
  28.9 95.1 %all-gather = s32[128,1,64]{2,1,0:T(1,128)S(1)} all-gather(s32[1,1,64]{2,1,0:T(1,128)} %bitcast.584), channel_id=1, replica_groups=mesh['pool'=128,'tp'=4] {'pool'}, dimensions={0}, use_global_device_ids=true | all-gather | bytes 33024 | tf_op jit(solution)/shard_map/all_gather | solution.py:31
  124.1 33.1 %gather_fusion = bf16[8192,256]{1,0:T(8,128)(2,1)} fusion(bf16[1024,256]{1,0:T(8,128)(2,1)S(1)} %bitcast.577, s32[8192]{0:T(1024)S(1)} %broadcast_clamp_fusion), kind=kCustom, calls=%fused_computation | custom fusion | bytes 8421376 | tf_op jit(solution)/shard_map/jit(_take)/gather | solution.py:32
  157.2 4.4 broadcast_select_fusion
  168.9 0.6 constant_dynamic-update-slice_fusion.115
  240.1 10.9 %all-to-all-start.1 = ((bf16[128,1,64,1,256]{4,2,3,1,0:T(8,128)(2,1)}), bf16[128,1,64,1,256]{4,2,3,1,0:T(8,128)(2,1)}, u32[]{:S(2)}, u32[]{:S(2)}) async-start(bf16[128,1,64,1,256]{4,2,3,1,0:T(8,128)(2,1)} %constant_dynamic-update-slice_fusion), calls=%async_computation.2 | async-start | bytes 8388608 | tf_op jit(solution)/shard_map/all_to_all | solution.py:34
  251.1 0.7 all-gather.3.cloned.1.call-update
  252.0 184.2 %all-gather.3.cloned.1.call-done = bf16[2048,1024]{0,1:T(8,128)(2,1)} async-done(((bf16[2048,8]{0,1:T(8,128)(2,1)}), bf16[2048,1024]{0,1:T(8,128)(2,1)}) %all-gather.3.cloned.1.call-update) | async-done | bytes 4194320 | tf_op jit(solution)/shard_map/all_gather | solution.py:23
  436.1 4.4 convolution_convert_fusion
  440.8 28.9 %reduce-scatter.2.cloned.1.call-done = bf16[128,256]{1,0:T(8,128)(2,1)} async-done(((bf16[128,1024]{1,0:T(8,128)(2,1)}), bf16[128,256]{1,0:T(8,128)(2,1)}) %reduce-scatter.2.cloned.1.call-update) | async-done | bytes 65552 | tf_op jit(solution)/shard_map/reduce_scatter | solution.py:26
  469.7 1.0 select_reduce_fusion
  470.8 1.0 fusion.12
  471.9 6.5 %copy.20 = bf16[1,64,128,1,256]{4,2,1,3,0:T(8,128)(2,1)} copy(bf16[1,64,128,1,256]{4,1,3,0,2:T(8,128)(2,1)} %bitcast.136) | data formatting | bytes 8388608 | tf_op jit(solution)/shard_map/reshape | solution.py:33
  478.4 31.4 %while.15 = (s32[]{:T(128)}, f32[1024]{0:T(1024)S(1)}, f32[1024]{0:T(1024)S(1)}, f32[1024,128]{1,0:T(8,128)S(1)}, s32[8,2,8]{2,0,1:T(8,128)S(1)}, /*index=5*/bf1...) while((s32[]{:T(128)}, f32[1024]{0:T(1024)S(1)}, ...), condition=%wide.region_7.8_spmd.clone, body=%wide.region_3.7_spmd.clone.sunk | while | flops 545550336 | bytes 15561029 | solution.py:82
  478.5 1.1 dynamic-slice_bitcast_fusion.2
  479.6 0.7 fusion.38
  480.3 0.9 fusion.39
  481.3 1.0 convolution_add_fusion.2
  482.4 1.1 dynamic-slice_bitcast_fusion.2
  483.5 0.7 fusion.38
  484.3 0.9 fusion.39
  485.2 1.0 convolution_add_fusion.2
  486.4 1.1 dynamic-slice_bitcast_fusion.2
  487.5 0.7 fusion.38
  488.2 0.9 fusion.39
  489.2 1.0 convolution_add_fusion.2
  490.3 1.1 dynamic-slice_bitcast_fusion.2
  491.4 0.7 fusion.38
  492.1 0.9 fusion.39
  493.1 1.0 convolution_add_fusion.2
  494.2 1.1 dynamic-slice_bitcast_fusion.2
  495.3 0.7 fusion.38
  496.1 0.9 fusion.39
  497.0 1.0 convolution_add_fusion.2
  498.2 1.1 dynamic-slice_bitcast_fusion.2
  499.2 0.7 fusion.38
  500.0 0.9 fusion.39
  501.0 1.0 convolution_add_fusion.2
  502.1 1.1 dynamic-slice_bitcast_fusion.2
  503.2 0.7 fusion.38
  503.9 0.9 fusion.39
  504.9 1.0 convolution_add_fusion.2
  506.0 1.1 dynamic-slice_bitcast_fusion.2
  507.1 0.7 fusion.38
  507.9 0.9 fusion.39
  508.8 1.0 convolution_add_fusion.2
  510.0 0.8 convert_element_type.18
  (204 shorter events, 79.7 us)
Async XLA Ops:
  7.2 429.0 %copy-start = (bf16[128,2048]{1,0:T(8,128)(2,1)S(1)}, bf16[128,2048]{1,0:T(8,128)(2,1)}, u32[]{:S(2)}) copy-start(bf16[128,2048]{1,0:T(8,128)(2,1)} %param.8) | copy-start | bytes 1572868
  9.4 114.7 %all-to-all-start = ((bf16[8,128,256]{2,0,1:T(8,128)(2,1)}), bf16[8,128,256]{2,0,1:T(8,128)(2,1)S(1)}, u32[]{:S(2)}, u32[]{:S(2)}) async-start(bf16[8,128,256]{2,0,1:T(8,128)(2,1)} %copy.19), calls=%async_computation.1 | async-start | bytes 1048576 | tf_op jit(solution)/shard_map/all_to_all | solution.py:29
  240.1 231.8 %all-to-all-start.1 = ((bf16[128,1,64,1,256]{4,2,3,1,0:T(8,128)(2,1)}), bf16[128,1,64,1,256]{4,2,3,1,0:T(8,128)(2,1)}, u32[]{:S(2)}, u32[]{:S(2)}) async-start(bf16[128,1,64,1,256]{4,2,3,1,0:T(8,128)(2,1)} %constant_dynamic-update-slice_fusion), calls=%async_computation.2 | async-start | bytes 8388608 | tf_op jit(solution)/shard_map/all_to_all | solution.py:34
  251.0 189.6 %copy-start.1 = (bf16[128,1024]{1,0:T(8,128)(2,1)S(1)}, bf16[128,1024]{1,0:T(8,128)(2,1)}, u32[]{:S(2)}) copy-start(bf16[128,1024]{1,0:T(8,128)(2,1)} %param.10) | copy-start | bytes 786436
  251.0 189.7 %copy-start.2 = (s32[1,2,64]{2,1,0:T(2,128)S(1)}, s32[1,2,64]{2,1,0:T(2,128)}, u32[]{:S(2)}) copy-start(s32[1,2,64]{2,1,0:T(2,128)} %param.13) | copy-start | bytes 1540
  251.0 185.1 %all-gather.3.cloned.1.call-start = ((), (), s32[]{:S(2)}) async-start(), calls=%async_computation.3 | async-start | bytes 4227072 | tf_op jit(solution)/shard_map/all_gather | solution.py:23
  251.8 217.9 %reduce-scatter.2.cloned.1.call-start = ((), (), s32[]{:S(2)}) async-start(), calls=%async_computation.4 | async-start | bytes 327680 | tf_op jit(solution)/shard_map/reduce_scatter | solution.py:26
Sparse Core Ops, SparseCore 0:
  255.0 181.1 all-gather.2
  440.7 28.9 reduce-scatter.1
